TPU v7x, 128 devices: a whole 4x4x4 slice. The times are simulated.
128 devices in a mesh: dp: 4 (over x), tensor: 32 (over z, y, core).
Axes of the slice: x: 4, y: 4, z: 4, core: 2. Of those that a mesh axis runs over, the one named last changes fastest.
Arguments:
- inputs: bfloat16 [1024, 28672], P('dp', 'tensor'), may hold values from -0.1875 to 0.1875
- output_gradient: bfloat16 [1024, 8192], P('dp', 'tensor'), may hold values from -6 to 6
- frozen: bfloat16 [8192, 28672], P('dp', 'tensor'), may hold values from -0.5905695 to 0.5905695
- adapter_down_factor: bfloat16 [64, 28672], P(None, 'tensor'), may hold values from -0.03125 to 0.03125
- adapter_up_factor: bfloat16 [8192, 64], P('dp'), may hold values from -0.3125 to 0.3125
- magnitude: float32 [8192], P('dp'), may hold values from 0.5 to 2
Outputs:
- input_gradient_rows: bfloat16 [1024, 28672], P('dp', 'tensor')
- adapter_down_gradient: float32 [64, 28672], P(None, 'tensor')
- adapter_up_gradient: float32 [8192, 64], P('dp')
- magnitude_gradient: float32 [8192], P('dp')
All inputs are finite; a program needn't handle non-finite values.
Results may differ from a plain program's by a relative error of at most 0.0057.
Values may be sent and summed in bfloat16 or wider, within the bound.
No kernel may reach another device: no remote copies, remote signals or barrier semaphores. Data moves between devices by JAX's collectives and lax.ppermute only.
A program may use at most 128 MiB of HBM per device.

v0:
```python
import jax
import jax.numpy as jnp
from jax import lax
from jax.sharding import PartitionSpec as P

adapter_scale = 2.0
epsilon = 1e-06


def local(inputs, output_gradient, frozen, adapter_down_factor, adapter_up_factor, magnitude):
    full_grad = lax.all_gather(output_gradient, "tensor", axis=1, tiled=True)
    row_grad = lax.all_to_all(full_grad, "dp", split_axis=1, concat_axis=0, tiled=True)
    combined_weight = frozen.astype(jnp.float32) + adapter_scale * jnp.dot(
        adapter_up_factor, adapter_down_factor, preferred_element_type=jnp.float32
    )
    merged_b = combined_weight.astype(jnp.bfloat16)
    squares = jnp.sum(combined_weight * combined_weight, axis=1)
    total_squares = lax.psum(squares, "tensor")
    weight_row_norm = jnp.sqrt(total_squares + epsilon)
    col_scale = magnitude / weight_row_norm
    scaled_rows = (row_grad.astype(jnp.float32) * col_scale[None, :]).astype(jnp.bfloat16)
    summed = lax.psum_scatter(
        jnp.dot(scaled_rows, merged_b, preferred_element_type=jnp.float32),
        "dp",
        scatter_dimension=0,
        tiled=True,
    )
    input_gradient_rows = summed.astype(jnp.bfloat16)
    product = lax.dot_general(
        row_grad,
        lax.all_gather(inputs, "dp", axis=0, tiled=True),
        (((0,), (0,)), ((), ())),
        preferred_element_type=jnp.float32,
    )
    gradient_row_sums = lax.psum(jnp.sum(product * combined_weight, axis=1), "tensor")
    combined_weight_gradient = col_scale[:, None] * product
    down_partial_sum = adapter_scale * lax.dot_general(
        adapter_up_factor.astype(jnp.float32),
        combined_weight_gradient,
        (((0,), (0,)), ((), ())),
        precision=lax.Precision.HIGHEST,
    )
    adapter_down_gradient = lax.psum(down_partial_sum, "dp")
    up_partial_sum = adapter_scale * jnp.dot(
        combined_weight_gradient,
        adapter_down_factor.astype(jnp.float32).T,
        precision=lax.Precision.HIGHEST,
    )
    adapter_up_gradient = lax.psum(up_partial_sum, "tensor")
    magnitude_gradient = gradient_row_sums / weight_row_norm
    return (input_gradient_rows, adapter_down_gradient, adapter_up_gradient, magnitude_gradient)


def solution(mesh):
    placed = (
        P("dp", "tensor"),
        P("dp", "tensor"),
        P("dp", "tensor"),
        P(None, "tensor"),
        P("dp", None),
        P("dp"),
    )
    return jax.shard_map(
        local,
        mesh=mesh,
        in_specs=placed,
        out_specs=(P("dp", "tensor"), P(None, "tensor"), P("dp", None), P("dp")),
        check_vma=False,
    )
```

profile of v0, /device:TPU:1, one launch (start us, length us, event | category | flops | bytes accessed | tf_op | source)
XLA Modules:
  0.0 486.6 jit_solution(599287304383377299)
XLA Ops:
  8.1 1.7 copy.12
  9.8 51.7 %all-gather.3.cloned.1.call-done = bf16[256,8192]{0,1:T(8,128)(2,1)} async-done(((bf16[256,256]{0,1:T(8,128)(2,1)}), bf16[256,8192]{0,1:T(8,128)(2,1)}) %all-gather.3.cloned.1.call-update) | async-done | bytes 4194320 | tf_op jit(solution)/shard_map/all_gather | solution.py:11
  61.5 5.0 %all-to-all-start = ((bf16[256,4,2048]{0,2,1:T(8,128)(2,1)}), bf16[256,4,2048]{0,2,1:T(8,128)(2,1)}, u32[]{:S(2)}, u32[]{:S(2)}) async-start(bf16[256,4,2048]{0,2,1:T(8,128)(2,1)} %bitcast.11), calls=%async_computation | async-start | bytes 8388608 | tf_op jit(solution)/shard_map/all_to_all | solution.py:12
  66.5 0.0 all-gather.5.cloned.1.call-start
  66.5 0.5 all-gather.5.cloned.1.call-update
  67.1 0.0 reduce-scatter.2.cloned.1.call-start
  67.1 6.2 %copy.14 = bf16[2048,896]{0,1:T(8,128)(2,1)} copy(bf16[2048,896]{1,0:T(8,128)(2,1)} %param.8) | data formatting | bytes 7340032 | tf_op args[2]
  73.3 6.1 %multiply_add_fusion = f32[2048,896]{0,1:T(8,128)} fusion(bf16[2048,896]{0,1:T(8,128)(2,1)} %copy.14, bf16[2048,64]{0,1:T(8,128)(2,1)S(1)} %copy-done, bf16[64,896]{1,0:T(8,128)(2,1)S(1)} %copy-done.1), kind=kOutput, calls=%fused_computation.3 | convolution fusion | flops 240386048 | bytes 11386880 | tf_op jit(solution)/shard_map/dot_general | solution.py:13
  79.4 50.5 %all-to-all-done = bf16[256,4,2048]{0,2,1:T(8,128)(2,1)} async-done(((bf16[256,4,2048]{0,2,1:T(8,128)(2,1)}), bf16[256,4,2048]{0,2,1:T(8,128)(2,1)}, u32[]{:S(2)}, u32[]{:S(2)}) %all-to-all-start) | async-done | bytes 4194336 | tf_op jit(solution)/shard_map/all_to_all | solution.py:12
  129.9 6.3 %copy.13 = bf16[4,256,2048]{2,1,0:T(8,128)(2,1)} copy(bf16[4,256,2048]{1,2,0:T(8,128)(2,1)} %bitcast.1) | data formatting | bytes 8388608 | tf_op jit(solution)/shard_map/all_to_all | solution.py:12
  136.2 12.5 %multiply_reduce_fusion = (f32[2048]{0:T(1024)S(1)}, f32[2048]{0:T(1024)S(1)}, f32[2048,896]{0,1:T(8,128)}) fusion(f32[2048,896]{0,1:T(8,128)} %multiply_add_fusion, bf16[1024,2048]{1,0:T(8,128)(2,1)} %bitcast.12, bf16[1024,896]{1,0:T(8,128)(2,1)} %all-gather.5.cloned.1.call-done), kind=kOutput, calls=%fused_computation.1 | convolution fusion | flops 3765432320 | bytes 20725760 | tf_op jit(solution)/shard_map/dot_general | solution.py:29
  148.7 120.9 %all-reduce = (f32[2048]{0:T(1024)S(1)}, f32[2048]{0:T(1024)S(1)}) all-reduce(f32[2048]{0:T(1024)S(1)} %get-tuple-element.5, f32[2048]{0:T(1024)S(1)} %get-tuple-element.4), channel_id=1, replica_groups=mesh['dp'=4,'tensor'=32] {'tensor'}, use_global_device_ids=true, to_apply=%region_1.0 | all-reduce | flops 4096 | bytes 32768 | tf_op jit(solution)/shard_map/psum | solution.py:18
  269.6 0.6 fusion.18
  270.2 10.7 %fusion.4 = f32[1024,896]{1,0:T(8,128)} fusion(bf16[1024,2048]{1,0:T(8,128)(2,1)} %bitcast.13, f32[2048]{0:T(1024)S(1)} %get-tuple-element.9, f32[2048,896]{0,1:T(8,128)} %multiply_add_fusion), kind=kOutput, calls=%fused_computation.8 | convolution fusion | flops 3766222848 | bytes 15212544 | tf_op jit(solution)/shard_map/dot_general | solution.py:23
  281.0 0.2 all-reduce.4.cloned.1.call-start
  281.2 7.8 %fusion.15 = f32[64,896]{1,0:T(8,128)} fusion(bf16[2048,64]{0,1:T(8,128)(2,1)S(1)} %copy-done, f32[2048,896]{0,1:T(8,128)} %get-tuple-element.10, f32[2048]{0:T(1024)S(1)} %get-tuple-element.9), kind=kOutput, calls=%fused_computation.15 | convolution fusion | flops 1411178496 | bytes 7839744 | tf_op jit(solution)/shard_map/dot_general | solution.py:37
  289.0 0.0 all-reduce.6.cloned.1.call-start
  289.1 7.4 %fusion.9 = f32[2048,64]{0,1:T(8,128)} fusion(bf16[64,896]{1,0:T(8,128)(2,1)S(1)} %copy-done.1, f32[2048,896]{0,1:T(8,128)} %get-tuple-element.10, f32[2048]{0:T(1024)S(1)} %get-tuple-element.9), kind=kOutput, calls=%fused_computation.13 | convolution fusion | flops 1411252224 | bytes 7987200 | tf_op jit(solution)/shard_map/dot_general | solution.py:44
  296.5 26.3 %reduce-scatter.2.cloned.1.call-done = f32[256,896]{1,0:T(8,128)} async-done(((f32[1024,896]{1,0:T(8,128)}), f32[256,896]{1,0:T(8,128)}) %reduce-scatter.2.cloned.1.call-update) | async-done | bytes 917520 | tf_op jit(solution)/shard_map/reduce_scatter | solution.py:22
  322.8 2.0 convert_element_type.21
  324.8 40.2 %all-reduce.4.cloned.1.call-done = f32[64,896]{1,0:T(8,128)} async-done(((f32[64,896]{1,0:T(8,128)}), f32[64,896]{1,0:T(8,128)}) %all-reduce.4.cloned.1.call-update) | async-done | bytes 229392 | tf_op jit(solution)/shard_map/psum | solution.py:43
  365.0 110.5 %all-reduce.6.cloned.1.call-done = f32[2048,64]{0,1:T(8,128)} async-done(((f32[2048,64]{0,1:T(8,128)}), f32[2048,64]{0,1:T(8,128)}) %all-reduce.6.cloned.1.call-update) | async-done | bytes 524304 | tf_op jit(solution)/shard_map/psum | solution.py:49
  475.4 1.6 copy.17
  477.1 1.9 copy.18
  (12 shorter events, 0.1 us)
Async XLA Ops:
  8.0 65.3 %copy-start = (bf16[2048,64]{0,1:T(8,128)(2,1)S(1)}, bf16[2048,64]{0,1:T(8,128)(2,1)}, u32[]{:S(2)}) copy-start(bf16[2048,64]{0,1:T(8,128)(2,1)} %param.10) | copy-start | bytes 786436
  8.0 53.5 %all-gather.3.cloned.1.call-start = ((), (), s32[]{:S(2)}) async-start(), calls=%async_computation.2 | async-start | bytes 4325376 | tf_op jit(solution)/shard_map/all_gather | solution.py:11
  61.5 11.8 %copy-start.1 = (bf16[64,896]{1,0:T(8,128)(2,1)S(1)}, bf16[64,896]{1,0:T(8,128)(2,1)}, u32[]{:S(2)}) copy-start(bf16[64,896]{1,0:T(8,128)(2,1)} %param.9) | copy-start | bytes 344068
  61.5 68.4 %all-to-all-start = ((bf16[256,4,2048]{0,2,1:T(8,128)(2,1)}), bf16[256,4,2048]{0,2,1:T(8,128)(2,1)}, u32[]{:S(2)}, u32[]{:S(2)}) async-start(bf16[256,4,2048]{0,2,1:T(8,128)(2,1)} %bitcast.11), calls=%async_computation | async-start | bytes 8388608 | tf_op jit(solution)/shard_map/all_to_all | solution.py:12
  66.5 69.7 %all-gather.5.cloned.1.call-start = ((), (), s32[]{:S(2)}) async-start(), calls=%async_computation.4 | async-start | bytes 2293760 | tf_op jit(solution)/shard_map/all_gather | solution.py:31
  67.1 255.7 %reduce-scatter.2.cloned.1.call-start = ((), (), s32[]{:S(2)}) async-start(), calls=%async_computation.3 | async-start | bytes 4587520 | tf_op jit(solution)/shard_map/reduce_scatter | solution.py:22
  136.2 133.4 %copy-start.2 = (f32[2048]{0:T(1024)S(1)}, f32[2048]{0:T(1024)}, u32[]{:S(2)}) copy-start(f32[2048]{0:T(1024)} %param.11) | copy-start | bytes 24580
  281.0 84.0 %all-reduce.4.cloned.1.call-start = ((), (), s32[]{:S(2)}) async-start(), calls=%async_computation.5 | async-start | bytes 458752 | tf_op jit(solution)/shard_map/psum | solution.py:43
  289.0 186.4 %all-reduce.6.cloned.1.call-start = ((), (), s32[]{:S(2)}) async-start(), calls=%async_computation.6 | async-start | bytes 1048576 | tf_op jit(solution)/shard_map/psum | solution.py:49
Sparse Core Ops, SparseCore 0:
  11.7 49.7 all-gather.2
Sparse Core Ops, SparseCore 1:
  68.6 42.3 all-gather.4
  281.1 41.7 reduce-scatter.1
  325.6 39.3 all-reduce.3
  368.8 106.6 all-reduce.5
where the time goes:
time: 487 us
  waiting for transfers between devices  280 us (57%)
  blocking collectives  121 us (25%)
  matrix products  44.6 us (9%)
  local copies, waits for them, and re-layouts  17.7 us (4%)
  between operations  15.7 us (3%)
  starting transfers between devices  5.4 us (1%)
    psum x1, blocking collectives, local(): total_squares = lax.psum(squares, 'tensor')  121 us
    psum x1, waiting for transfers between devices, local(): adapter_up_gradient = lax.psum(up_partial_sum, 'tensor')  110 us
    all_gather x1, waiting for transfers between devices, local(): full_grad = lax.all_gather(output_gradient, 'tensor', axis=1, tiled=True)  51.7 us
    all_to_all x1, waiting for transfers between devices, local(): lax.all_to_all(full_grad, 'dp', split_axis=1, concat_axis=0, tiled=True)  50.5 us
    psum x1, waiting for transfers between devices, local(): adapter_down_gradient = lax.psum(down_partial_sum, 'dp')  40.2 us
    reduce_scatter x1, waiting for transfers between devices, local(): lax.psum_scatter(jnp.dot(scaled_rows, merged_b, preferred_element_type=jn...  26.3 us
    dot_general x1, matrix products, local(): lax.dot_general(row_grad, lax.all_gather(inputs, 'dp', axis=0, tiled=True...  12.5 us
    unnamed x10, local copies, waits for them, and re-layouts  11.4 us
  transfers between devices with their start and end apart: 6, of which 5 were waited for; matrix products, arithmetic and copies ran while one was open for 7% of the time, Pallas kernels for 0%

commit v1 on v0

--- a/solution.py
+++ b/solution.py
@@ -1,3 +1,4 @@
+import functools
 import jax
 import jax.numpy as jnp
 from jax import lax
@@ -5,6 +6,13 @@
 
 adapter_scale = 2.0
 epsilon = 1e-06
+
+
+def _place_stacks_all(z, which_axis):
+    return jax.lax.all_gather(z, axis_name=which_axis).sum(axis=0)
+
+
+treat_targets = functools.partial(_place_stacks_all, which_axis="tensor")
 
 
 def local(inputs, output_gradient, frozen, adapter_down_factor, adapter_up_factor, magnitude):
@@ -46,7 +54,7 @@
         adapter_down_factor.astype(jnp.float32).T,
         precision=lax.Precision.HIGHEST,
     )
-    adapter_up_gradient = lax.psum(up_partial_sum, "tensor")
+    adapter_up_gradient = treat_targets(up_partial_sum)
     magnitude_gradient = gradient_row_sums / weight_row_norm
     return (input_gradient_rows, adapter_down_gradient, adapter_up_gradient, magnitude_gradient)
 

time: 487 us -> 398 us (0.82)
  waiting for transfers between devices: 280 us -> 165 us
  local copies, waits for them, and re-layouts: 17.7 us -> 33.5 us
  other arithmetic: 2.61 us -> 12.2 us
    psum x1 -> x0, waiting for transfers between devices: 110 us -> none  [local(): adapter_up_gradient = lax.psum(up_partial_sum, 'tensor')]
    psum x1, waiting for transfers between devices: 40.2 us -> 0.01 us  [local(): adapter_down_gradient = lax.psum(down_partial_sum, 'dp')]
    all_gather x0 -> x1, waiting for transfers between devices: none -> 36 us  [_place_stacks_all(): return jax.lax.all_gather(z, axis_name=which_axis).sum(axis=0)]
    unnamed x10, local copies, waits for them, and re-layouts: 11.4 us -> 27.2 us
    reduce_sum x0 -> x1, other arithmetic: none -> 9.55 us  [_place_stacks_all(): return jax.lax.all_gather(z, axis_name=which_axis).sum(axis=0)]
  transfers between devices with their start and end apart: 6 -> 6, of which waited for: 5 -> 4; matrix products, arithmetic and copies ran while one was open for 7% -> 16% of each run, Pallas kernels for 0% -> 0%
where the time goes in v1:
time: 398 us; the launch traced here: 397 us
  waiting for transfers between devices  165 us (41%)
  blocking collectives  121 us (30%)
  matrix products  44.8 us (11%)
  local copies, waits for them, and re-layouts  33.5 us (8%)
  between operations  15.7 us (4%)
  other arithmetic  12.2 us (3%)
  starting transfers between devices  5.4 us (1%)
    psum x1, blocking collectives, local(): total_squares = lax.psum(squares, 'tensor')  121 us
    all_gather x1, waiting for transfers between devices, local(): full_grad = lax.all_gather(output_gradient, 'tensor', axis=1, tiled=True)  51.7 us
    all_to_all x1, waiting for transfers between devices, local(): lax.all_to_all(full_grad, 'dp', split_axis=1, concat_axis=0, tiled=True)  50.5 us
    all_gather x1, waiting for transfers between devices, _place_stacks_all(): return jax.lax.all_gather(z, axis_name=which_axis).sum(axis=0)  36 us
    unnamed x10, local copies, waits for them, and re-layouts  27.2 us
    reduce_scatter x1, waiting for transfers between devices, local(): lax.psum_scatter(jnp.dot(scaled_rows, merged_b, preferred_element_type=jn...  26 us
    dot_general x1, matrix products, local(): lax.dot_general(row_grad, lax.all_gather(inputs, 'dp', axis=0, tiled=True...  12.4 us
    dot_general x1, matrix products, local(): jnp.dot(scaled_rows, merged_b, preferred_element_type=jnp.float32)  10.8 us
  transfers between devices with their start and end apart: 6, of which 4 were waited for; matrix products, arithmetic and copies ran while one was open for 16% of the time, Pallas kernels for 0%

profile of v1, /device:TPU:1, one launch (start us, length us, event | category | flops | bytes accessed | tf_op | source)
XLA Modules:
  0.0 397.3 jit_solution(17612344878268518882)
XLA Ops:
  8.1 1.7 copy.12
  9.8 51.7 %all-gather.5.cloned.1.call-done = bf16[256,8192]{0,1:T(8,128)(2,1)} async-done(((bf16[256,256]{0,1:T(8,128)(2,1)}), bf16[256,8192]{0,1:T(8,128)(2,1)}) %all-gather.5.cloned.1.call-update) | async-done | bytes 4194320 | tf_op jit(solution)/shard_map/all_gather | solution.py:19
  61.5 5.0 %all-to-all-start = ((bf16[256,4,2048]{0,2,1:T(8,128)(2,1)}), bf16[256,4,2048]{0,2,1:T(8,128)(2,1)}, u32[]{:S(2)}, u32[]{:S(2)}) async-start(bf16[256,4,2048]{0,2,1:T(8,128)(2,1)} %bitcast.17), calls=%async_computation | async-start | bytes 8388608 | tf_op jit(solution)/shard_map/all_to_all | solution.py:20
  66.5 0.0 all-gather.7.cloned.1.call-start
  66.5 0.5 all-gather.7.cloned.1.call-update
  67.1 0.0 reduce-scatter.2.cloned.1.call-start
  67.1 6.2 %copy.14 = bf16[2048,896]{0,1:T(8,128)(2,1)} copy(bf16[2048,896]{1,0:T(8,128)(2,1)} %param.8) | data formatting | bytes 7340032 | tf_op args[2]
  73.3 6.1 %multiply_add_fusion = f32[2048,896]{0,1:T(8,128)} fusion(bf16[2048,896]{0,1:T(8,128)(2,1)} %copy.14, bf16[2048,64]{0,1:T(8,128)(2,1)S(1)} %copy-done, bf16[64,896]{1,0:T(8,128)(2,1)S(1)} %copy-done.1), kind=kOutput, calls=%fused_computation.4 | convolution fusion | flops 240386048 | bytes 11386880 | tf_op jit(solution)/shard_map/dot_general | solution.py:21
  79.4 50.5 %all-to-all-done = bf16[256,4,2048]{0,2,1:T(8,128)(2,1)} async-done(((bf16[256,4,2048]{0,2,1:T(8,128)(2,1)}), bf16[256,4,2048]{0,2,1:T(8,128)(2,1)}, u32[]{:S(2)}, u32[]{:S(2)}) %all-to-all-start) | async-done | bytes 4194336 | tf_op jit(solution)/shard_map/all_to_all | solution.py:20
  129.9 6.3 %copy.13 = bf16[4,256,2048]{2,1,0:T(8,128)(2,1)} copy(bf16[4,256,2048]{1,2,0:T(8,128)(2,1)} %bitcast.1) | data formatting | bytes 8388608 | tf_op jit(solution)/shard_map/all_to_all | solution.py:20
  136.2 12.4 %multiply_reduce_fusion = (f32[2048]{0:T(1024)S(1)}, f32[2048]{0:T(1024)S(1)}, f32[2048,896]{0,1:T(8,128)}) fusion(f32[2048,896]{0,1:T(8,128)} %multiply_add_fusion, bf16[1024,2048]{1,0:T(8,128)(2,1)} %bitcast.18, bf16[1024,896]{1,0:T(8,128)(2,1)} %all-gather.7.cloned.1.call-done), kind=kOutput, calls=%fused_computation.2 | convolution fusion | flops 3765432320 | bytes 20725760 | tf_op jit(solution)/shard_map/dot_general | solution.py:37
  148.6 120.9 %all-reduce = (f32[2048]{0:T(1024)S(1)}, f32[2048]{0:T(1024)S(1)}) all-reduce(f32[2048]{0:T(1024)S(1)} %get-tuple-element.5, f32[2048]{0:T(1024)S(1)} %get-tuple-element.4), channel_id=1, replica_groups=mesh['dp'=4,'tensor'=32] {'tensor'}, use_global_device_ids=true, to_apply=%region_1.0 | all-reduce | flops 4096 | bytes 32768 | tf_op jit(solution)/shard_map/psum | solution.py:26
  269.5 0.6 fusion.18
  270.1 10.8 %fusion.4 = f32[1024,896]{1,0:T(8,128)} fusion(bf16[1024,2048]{1,0:T(8,128)(2,1)} %bitcast.19, f32[2048]{0:T(1024)S(1)} %get-tuple-element.9, f32[2048,896]{0,1:T(8,128)} %multiply_add_fusion), kind=kOutput, calls=%fused_computation.9 | convolution fusion | flops 3766222848 | bytes 15212544 | tf_op jit(solution)/shard_map/dot_general | solution.py:31
  280.9 0.2 all-gather.9.cloned.1.call-start
  281.2 7.0 %fusion.9 = f32[2048,64]{0,1:T(8,128)} fusion(bf16[64,896]{1,0:T(8,128)(2,1)S(1)} %copy-done.1, f32[2048,896]{0,1:T(8,128)} %get-tuple-element.10, f32[2048]{0:T(1024)S(1)} %get-tuple-element.9), kind=kOutput, calls=%fused_computation.14 | convolution fusion | flops 1411252224 | bytes 7987200 | tf_op jit(solution)/shard_map/dot_general | solution.py:52
  288.2 0.0 all-reduce.3.cloned.1.call-start
  288.2 8.5 %fusion.15 = f32[64,896]{1,0:T(8,128)} fusion(bf16[2048,64]{0,1:T(8,128)(2,1)S(1)} %copy-done, f32[2048,896]{0,1:T(8,128)} %get-tuple-element.10, f32[2048]{0:T(1024)S(1)} %get-tuple-element.9), kind=kOutput, calls=%fused_computation.16 | convolution fusion | flops 1411178496 | bytes 7839744 | tf_op jit(solution)/shard_map/dot_general | solution.py:45
  296.7 26.0 %reduce-scatter.2.cloned.1.call-done = f32[256,896]{1,0:T(8,128)} async-done(((f32[1024,896]{1,0:T(8,128)}), f32[256,896]{1,0:T(8,128)}) %reduce-scatter.2.cloned.1.call-update) | async-done | bytes 917520 | tf_op jit(solution)/shard_map/reduce_scatter | solution.py:30
  322.8 2.0 convert_element_type.21
  324.8 36.0 %all-gather.9.cloned.1.call-done = f32[65536,64]{0,1:T(8,128)} async-done(((f32[2048,64]{0,1:T(8,128)}), f32[65536,64]{0,1:T(8,128)}) %all-gather.9.cloned.1.call-update) | async-done | bytes 16777232 | tf_op jit(solution)/shard_map/all_gather | solution.py:12
  360.8 17.7 %copy.15 = f32[8,8,32,2048]{3,2,1,0:T(8,128)} copy(f32[8,8,32,2048]{3,1,2,0:T(8,128)} %bitcast.16) | data formatting | bytes 33554432
  378.5 9.6 %bitcast_reduce_fusion = f32[2048,64]{0,1:T(8,128)} fusion(f32[8,8,32,2048]{3,2,1,0:T(8,128)} %copy.15), kind=kLoop, calls=%fused_computation | loop fusion | flops 4063232 | bytes 17301504 | tf_op jit(solution)/shard_map/reduce_sum | solution.py:12
  388.0 1.6 copy.17
  (13 shorter events, 0.1 us)
Async XLA Ops:
  8.0 65.3 %copy-start = (bf16[2048,64]{0,1:T(8,128)(2,1)S(1)}, bf16[2048,64]{0,1:T(8,128)(2,1)}, u32[]{:S(2)}) copy-start(bf16[2048,64]{0,1:T(8,128)(2,1)} %param.10) | copy-start | bytes 786436
  8.0 53.5 %all-gather.5.cloned.1.call-start = ((), (), s32[]{:S(2)}) async-start(), calls=%async_computation.2 | async-start | bytes 4325376 | tf_op jit(solution)/shard_map/all_gather | solution.py:19
  61.5 11.8 %copy-start.1 = (bf16[64,896]{1,0:T(8,128)(2,1)S(1)}, bf16[64,896]{1,0:T(8,128)(2,1)}, u32[]{:S(2)}) copy-start(bf16[64,896]{1,0:T(8,128)(2,1)} %param.9) | copy-start | bytes 344068
  61.5 68.4 %all-to-all-start = ((bf16[256,4,2048]{0,2,1:T(8,128)(2,1)}), bf16[256,4,2048]{0,2,1:T(8,128)(2,1)}, u32[]{:S(2)}, u32[]{:S(2)}) async-start(bf16[256,4,2048]{0,2,1:T(8,128)(2,1)} %bitcast.17), calls=%async_computation | async-start | bytes 8388608 | tf_op jit(solution)/shard_map/all_to_all | solution.py:20
  66.5 69.7 %all-gather.7.cloned.1.call-start = ((), (), s32[]{:S(2)}) async-start(), calls=%async_computation.4 | async-start | bytes 2293760 | tf_op jit(solution)/shard_map/all_gather | solution.py:39
  67.1 255.7 %reduce-scatter.2.cloned.1.call-start = ((), (), s32[]{:S(2)}) async-start(), calls=%async_computation.3 | async-start | bytes 4587520 | tf_op jit(solution)/shard_map/reduce_scatter | solution.py:30
  136.2 133.3 %copy-start.2 = (f32[2048]{0:T(1024)S(1)}, f32[2048]{0:T(1024)}, u32[]{:S(2)}) copy-start(f32[2048]{0:T(1024)} %param.11) | copy-start | bytes 24580
  280.9 79.9 %all-gather.9.cloned.1.call-start = ((), (), s32[]{:S(2)}) async-start(), calls=%async_computation.6 | async-start | bytes 17301504 | tf_op jit(solution)/shard_map/all_gather | solution.py:12
  288.2 99.9 %all-reduce.3.cloned.1.call-start = ((), (), s32[]{:S(2)}) async-start(), calls=%async_computation.5 | async-start | bytes 458752 | tf_op jit(solution)/shard_map/psum | solution.py:51
Sparse Core Ops, SparseCore 0:
  11.7 49.7 all-gather.4
  288.3 72.4 all-gather.8
Sparse Core Ops, SparseCore 1:
  68.6 42.3 all-gather.6
  281.0 41.7 reduce-scatter.1
  325.5 39.3 all-reduce.2
